TPU v7x, 256 devices: a whole 4x4x8 slice. The times are simulated.
256 devices in a mesh: dp: 64 (over z, y, core), mp: 4 (over x).
Axes of the slice: x: 4, y: 4, z: 8, core: 2. Of those that a mesh axis runs over, the one named last changes fastest.
Arguments:
- tree_query: bfloat16 [8192, 2048], P('dp', 'mp'), may hold values from -6 to 6
- new_kv: bfloat16 [8192, 2, 512], P('dp', None, 'mp'), may hold values from -6 to 6
- kv_cache: bfloat16 [2560, 2, 128, 512], P('dp', None, None, 'mp'), may hold values from -4 to 4
- page_table: int32 [128, 32], P('dp'), may hold values from 0 to 39, as said below
- cache_len: int32 [128], P('dp'), may hold values from 2 to 4096, as said below
- tree_mask: int32 [128, 64, 64], P('dp'), may hold values from 0 to 1, as said below
- out_weight: bfloat16 [2048, 2048], P('mp'), may hold values from -0.5 to 0.5
- residual_in: bfloat16 [8192, 2048], P('dp'), may hold values from -3 to 3
- norm_gain: float32 [2048], replicated, may hold values from 0.25 to 1.75
- route_ids: int32 [8192, 6], P('dp'), may hold values from 0 to 63, all different within a row; in each aligned block of 128 rows (0 to 127, 128 to 255, ...) at most 16 rows name the same one
- route_weight: float32 [8192, 6], P('dp'), may hold values from 0.05 to 0.5
- w_gate: bfloat16 [64, 2048, 1408], P('dp', None, 'mp'), may hold values from -0.125 to 0.125
- w_up: bfloat16 [64, 2048, 1408], P('dp', None, 'mp'), may hold values from -0.125 to 0.125
- w_down: bfloat16 [64, 1408, 2048], P('dp', None, 'mp'), may hold values from -0.15625 to 0.15625
- shared_gate: bfloat16 [2048, 2816], P('dp', 'mp'), may hold values from -0.125 to 0.125
- shared_up: bfloat16 [2048, 2816], P('dp', 'mp'), may hold values from -0.125 to 0.125
- shared_down: bfloat16 [2816, 2048], P('mp', 'dp'), may hold values from -0.109375 to 0.109375
Outputs:
- layer_out: bfloat16 [8192, 2048], P('dp', 'mp')
Inputs may be any that keep to these rules, and one draw needn't show every extreme that they name: `route_ids`: each row names 6 different experts. Within the rows of one index of dp (aligned blocks of 128 rows) no expert is named by more than 16 rows, and in some block one expert is named by exactly 16 rows. `cache_len`: the pages of the requests of one index of dp number at most 40 together; some request has exactly 4096 cached positions. `page_table`: entry [r, j] is the slot, in the pool of the index of dp that holds request r, of the page with cache positions j * 128 to j * 128 + 127. Entries with j * 128 < cache_len[r] are distinct over the requests of one index of dp; the other entries are valid slots whose contents are not read. tree_mask[r, i, u] is 1 where tree node u is node i or an ancestor of it, else 0; node 0 is the root and each other node's parent has a smaller index.
All inputs are finite; a program needn't handle non-finite values.
Results may differ from a plain program's by a relative error of at most 0.009.
Values may be sent and summed in bfloat16 or wider, within the bound.
No kernel may reach another device: no remote copies, remote signals or barrier semaphores. Data moves between devices by JAX's collectives and lax.ppermute only.
A program may use at most 128 MiB of HBM per device.

v0:
```python
import jax
import jax.numpy as jnp
from jax import lax
from jax.sharding import PartitionSpec as P

NEGATIVE_FILL = -1e30
EPSILON = 1e-05


def normalize(rows, gain):
    values = rows.astype(jnp.float32)
    mean_square = jnp.mean(values * values, axis=-1, keepdims=True)
    return (values * lax.rsqrt(mean_square + EPSILON) * gain).astype(jnp.bfloat16)


def attend_requests(
    queries, tree_keys, tree_values, tree_allow, kv_cache, page_table, cache_len, score_scale
):

    def per_request(request_item):
        q_rows, own_keys, own_values, allow_rows, table_row, length = request_item
        kv_pages = kv_cache[table_row]
        cache_keys = kv_pages[:, 0].reshape(-1, kv_pages.shape[-1])
        cache_values = kv_pages[:, 1].reshape(-1, kv_pages.shape[-1])
        live_mask = (jnp.arange(cache_keys.shape[0], dtype=jnp.int32) < length)[None, :]
        cache_scores = (
            jnp.einsum("qd,kd->qk", q_rows, cache_keys, preferred_element_type=jnp.float32)
            * score_scale
        )
        cache_scores = jnp.where(live_mask, cache_scores, NEGATIVE_FILL)
        tree_scores = (
            jnp.einsum("qd,ud->qu", q_rows, own_keys, preferred_element_type=jnp.float32)
            * score_scale
        )
        tree_scores = jnp.where(allow_rows, tree_scores, NEGATIVE_FILL)
        row_peak = jnp.maximum(jnp.max(cache_scores, axis=1), jnp.max(tree_scores, axis=1))[:, None]
        cache_probs = jnp.where(live_mask, jnp.exp(cache_scores - row_peak), 0.0)
        tree_probs = jnp.where(allow_rows, jnp.exp(tree_scores - row_peak), 0.0)
        denom_sum = jnp.sum(cache_probs, axis=1) + jnp.sum(tree_probs, axis=1)
        weighted = jnp.dot(
            cache_probs.astype(jnp.bfloat16), cache_values, preferred_element_type=jnp.float32
        )
        weighted = weighted + jnp.dot(
            tree_probs.astype(jnp.bfloat16), own_values, preferred_element_type=jnp.float32
        )
        return (weighted / denom_sum[:, None]).astype(jnp.bfloat16)

    return lax.map(
        per_request, (queries, tree_keys, tree_values, tree_allow, page_table, cache_len)
    )


def gather_mp(block, axis):
    parts = lax.axis_size("mp")
    copies = jnp.broadcast_to(block[None], (parts,) + block.shape)
    pieces = lax.all_to_all(copies, "mp", split_axis=0, concat_axis=0, tiled=True)
    pieces = jnp.moveaxis(pieces, 0, axis)
    shape = list(block.shape)
    shape[axis] = shape[axis] * parts
    return pieces.reshape(shape)


def scatter_sum_mp(terms):
    parts = lax.axis_size("mp")
    rows, width = terms.shape
    blocks = terms.reshape(rows, parts, width // parts).transpose(1, 0, 2)
    pieces = lax.all_to_all(blocks, "mp", split_axis=0, concat_axis=0, tiled=True)
    return jnp.sum(pieces.astype(jnp.float32), axis=0)


def run_experts(rows, w_gate, w_up, w_down):
    source_count, slot_count, model_width = rows.shape
    flat_rows = rows.reshape(source_count * slot_count, model_width)
    gate_proj = jnp.dot(flat_rows, w_gate[0], preferred_element_type=jnp.float32)
    up_proj = jnp.dot(flat_rows, w_up[0], preferred_element_type=jnp.float32)
    hidden_act = (jax.nn.silu(gate_proj) * up_proj).astype(jnp.bfloat16)
    down_rows = w_down[0]
    summed = jnp.dot(gather_mp(hidden_act, 1), down_rows, preferred_element_type=jnp.float32)
    outputs = summed.astype(jnp.bfloat16).reshape(source_count, slot_count, w_down.shape[2])
    return lax.all_to_all(outputs, "dp", split_axis=0, concat_axis=0, tiled=True)


def shared_experts(normed_rows, shared_gate, shared_up, shared_down):
    gate_total = jnp.dot(
        normed_rows,
        lax.all_gather(shared_gate, "dp", axis=0, tiled=True),
        preferred_element_type=jnp.float32,
    )
    up_total = jnp.dot(
        normed_rows,
        lax.all_gather(shared_up, "dp", axis=0, tiled=True),
        preferred_element_type=jnp.float32,
    )
    shared_hidden = (jax.nn.silu(gate_total) * up_total).astype(jnp.bfloat16)
    terms = jnp.dot(
        shared_hidden,
        lax.all_gather(shared_down, "dp", axis=1, tiled=True),
        preferred_element_type=jnp.float32,
    )
    return scatter_sum_mp(terms.astype(jnp.bfloat16))


def on_device(
    tree_query,
    new_kv,
    kv_cache,
    page_table,
    cache_len,
    tree_mask,
    out_weight,
    residual_in,
    norm_gain,
    route_ids,
    route_weight,
    w_gate,
    w_up,
    w_down,
    shared_gate,
    shared_up,
    shared_down,
):
    tok_rows = tree_query.shape[0]
    req_count = cache_len.shape[0]
    tree_len = tree_mask.shape[1]
    head_width = new_kv.shape[2]
    local_heads = tree_query.shape[1] // head_width
    score_scale = head_width ** (-0.5)
    queries = tree_query.reshape(req_count, tree_len, local_heads, head_width)
    queries = queries.transpose(0, 2, 1, 3).reshape(req_count, local_heads * tree_len, head_width)
    tree_keys = new_kv[:, 0, :].reshape(req_count, tree_len, head_width)
    tree_values = new_kv[:, 1, :].reshape(req_count, tree_len, head_width)
    tree_allow = jnp.tile(tree_mask, (1, local_heads, 1)) == 1
    attended = attend_requests(
        queries, tree_keys, tree_values, tree_allow, kv_cache, page_table, cache_len, score_scale
    )
    attended = attended.reshape(req_count, local_heads, tree_len, head_width).transpose(0, 2, 1, 3)
    attended = attended.reshape(tok_rows, local_heads * head_width)
    partial_value = jnp.dot(attended, out_weight, preferred_element_type=jnp.float32)
    model_width = residual_in.shape[1]
    quarter = model_width // lax.axis_size("mp")
    col_start = lax.axis_index("mp") * quarter
    experts = lax.axis_size("dp") * w_gate.shape[0]
    route_count = route_ids.shape[1]
    capacity = min(tok_rows, 4 * tok_rows * route_count // (3 * experts))
    expert_ids = route_ids.reshape(-1)
    onehot = (expert_ids[:, None] == jnp.arange(experts, dtype=jnp.int32)[None, :]).astype(
        jnp.int32
    )
    slot_index = jnp.sum((jnp.cumsum(onehot, axis=0) - onehot) * onehot, axis=1)
    own_residual = lax.dynamic_slice_in_dim(residual_in, col_start, quarter, 1)
    own_stream = (own_residual.astype(jnp.float32) + scatter_sum_mp(partial_value)).astype(
        jnp.bfloat16
    )
    stream = gather_mp(own_stream, 1)
    normed_rows = normalize(stream, norm_gain)
    codes = (expert_ids * capacity + slot_index).reshape(tok_rows, route_count)
    slots = jnp.arange(experts * capacity, dtype=jnp.int32)
    placing = jnp.any(codes[None, :, :] == slots[:, None, None], axis=2).astype(jnp.bfloat16)
    buffer = jnp.dot(placing, normed_rows, preferred_element_type=jnp.float32).astype(jnp.bfloat16)
    buffer = buffer.reshape(experts, capacity, normed_rows.shape[1])
    results = run_experts(
        lax.all_to_all(buffer, "dp", split_axis=0, concat_axis=0, tiled=True), w_gate, w_up, w_down
    )
    shared_out = shared_experts(normed_rows, shared_gate, shared_up, shared_down)
    result_rows = results.reshape(experts * capacity, quarter)
    picked = (
        result_rows[expert_ids * capacity + slot_index]
        .reshape(tok_rows, route_count, quarter)
        .astype(jnp.float32)
    )
    mixture = jnp.einsum("tk,tkc->tc", route_weight, picked, precision=lax.Precision.HIGHEST)
    return (own_stream.astype(jnp.float32) + shared_out.astype(jnp.float32) + mixture).astype(
        jnp.bfloat16
    )


def solution(mesh):
    return jax.shard_map(
        on_device,
        mesh=mesh,
        in_specs=(
            P("dp", "mp"),
            P("dp", None, "mp"),
            P("dp", None, None, "mp"),
            P("dp", None),
            P("dp"),
            P("dp", None, None),
            P("mp", None),
            P("dp", None),
            P(),
            P("dp", None),
            P("dp", None),
            P("dp", None, "mp"),
            P("dp", None, "mp"),
            P("dp", None, "mp"),
            P("dp", "mp"),
            P("dp", "mp"),
            P("mp", "dp"),
        ),
        out_specs=P("dp", "mp"),
        check_vma=False,
    )
```

profile of v0, /device:TPU:1, one launch (start us, length us, event | category | flops | bytes accessed | tf_op | source)
XLA Modules:
  0.0 334.9 jit_solution(15534831628222421942)
XLA Ops:
  13.0 18.3 %while.10 = (s32[]{:T(128)}, bf16[2,256,128]{2,1,0:T(8,128)(2,1)}, s32[2]{0:T(128)}, bf16[2,256,128]{2,1,0:T(8,128)(2,1)}, s32[2,32]{1,0:T(2,128)}, /*index=5*/b...) while((s32[]{:T(128)}, bf16[2,256,128]{2,1,0:T(8,128)(2,1)}, ...), condition=%wide.region_5.6_spmd, body=%wide.region_0.5_spmd.sunk | while | flops 554947200 | bytes 25811812 | solution.py:48
  13.7 2.7 gather_fusion
  22.8 2.7 gather_fusion
  33.0 2.9 copy.62
  35.8 2.7 convolution_bitcast_fusion
  38.6 4.8 %all-to-all-start = ((f32[4,128,512]{2,1,0:T(8,128)}), f32[4,128,512]{2,1,0:T(8,128)S(1)}, u32[]{:S(2)}, u32[]{:S(2)}) async-start(f32[4,128,512]{2,1,0:T(8,128)} %convolution_bitcast_fusion), calls=%async_computation | async-start | bytes 2097152 | tf_op jit(solution)/shard_map/all_to_all | solution.py:67
  46.7 9.9 %all-to-all-done = f32[4,128,512]{2,1,0:T(8,128)S(1)} async-done(((f32[4,128,512]{2,1,0:T(8,128)}), f32[4,128,512]{2,1,0:T(8,128)S(1)}, u32[]{:S(2)}, u32[]{:S(2)}) %all-to-all-start) | async-done | bytes 1048608 | tf_op jit(solution)/shard_map/all_to_all | solution.py:67
  58.6 3.5 %all-to-all-start.1 = ((bf16[4,128,512]{1,2,0:T(8,128)(2,1)}), bf16[4,128,512]{1,2,0:T(8,128)(2,1)S(1)}, u32[]{:S(2)}, u32[]{:S(2)}) async-start(bf16[4,128,512]{1,2,0:T(8,128)(2,1)} %broadcast_in_dim.54), calls=%async_computation.1 | async-start | bytes 1048576 | tf_op jit(solution)/shard_map/all_to_all | solution.py:56
  63.0 6.0 %all-to-all-done.1 = bf16[4,128,512]{1,2,0:T(8,128)(2,1)S(1)} async-done(((bf16[4,128,512]{1,2,0:T(8,128)(2,1)}), bf16[4,128,512]{1,2,0:T(8,128)(2,1)S(1)}, u32[]{:S(2)}, u32[]{:S(2)}) %all-to-all-start.1) | async-done | bytes 524320 | tf_op jit(solution)/shard_map/all_to_all | solution.py:56
  69.6 3.2 convolution_convert_fusion
  72.9 16.3 %all-to-all-start.3 = ((bf16[64,16,2048]{2,1,0:T(8,128)(2,1)}), bf16[64,16,2048]{2,1,0:T(8,128)(2,1)}, u32[]{:S(2)}, u32[]{:S(2)}) async-start(bf16[64,16,2048]{2,1,0:T(8,128)(2,1)} %bitcast.159), calls=%async_computation.3 | async-start | bytes 8388608 | tf_op jit(solution)/shard_map/all_to_all | solution.py:162
  89.9 102.8 %all-to-all-done.3 = bf16[64,16,2048]{2,1,0:T(8,128)(2,1)} async-done(((bf16[64,16,2048]{2,1,0:T(8,128)(2,1)}), bf16[64,16,2048]{2,1,0:T(8,128)(2,1)}, u32[]{:S(2)}, u32[]{:S(2)}) %all-to-all-start.3) | async-done | bytes 4194336 | tf_op jit(solution)/shard_map/all_to_all | solution.py:162
  192.7 4.4 %fusion.36 = f32[1024,352]{0,1:T(8,128)S(1)} fusion(bf16[1024,2048]{1,0:T(8,128)(2,1)} %bitcast.24, bf16[1,2048,352]{1,2,0:T(8,128)(2,1)} %param.30), kind=kOutput, calls=%fused_computation.50 | convolution fusion | flops 1476395008 | bytes 7077888 | tf_op jit(solution)/shard_map/dot_general | solution.py:74
  197.1 4.0 %fusion.38 = bf16[1024,352]{0,1:T(8,128)(2,1)S(1)} fusion(bf16[1024,2048]{1,0:T(8,128)(2,1)} %bitcast.24, bf16[1,2048,352]{1,2,0:T(8,128)(2,1)S(1)} %copy-done.10, f32[1024,352]{0,1:T(8,128)S(1)} %fusion.36), kind=kOutput, calls=%fused_computation.52 | convolution fusion | flops 1478557696 | bytes 7798784 | tf_op jit(solution)/shard_map/dot_general | solution.py:75
  203.2 4.6 %all-to-all-start.4 = ((bf16[4,1024,352]{1,2,0:T(8,128)(2,1)}), bf16[4,1024,352]{1,2,0:T(8,128)(2,1)}, u32[]{:S(2)}, u32[]{:S(2)}) async-start(bf16[4,1024,352]{1,2,0:T(8,128)(2,1)} %broadcast_in_dim.55), calls=%async_computation.4 | async-start | bytes 5767168 | tf_op jit(solution)/shard_map/all_to_all | solution.py:56
  207.8 3.2 fusion.62
  211.0 56.2 %all-gather.8.cloned.1.call-done = bf16[704,2048]{0,1:T(8,128)(2,1)} async-done(((bf16[704,32]{0,1:T(8,128)(2,1)}), bf16[704,2048]{0,1:T(8,128)(2,1)}) %all-gather.8.cloned.1.call-update) | async-done | bytes 2883600 | tf_op jit(solution)/shard_map/all_gather | solution.py:97
  267.2 6.2 %convolution_convert_fusion.1 = bf16[128,2048]{1,0:T(8,128)(2,1)S(1)} fusion(bf16[704,2048]{0,1:T(8,128)(2,1)} %all-gather.8.cloned.1.call-done, bf16[128,2048]{0,1:T(8,128)(2,1)S(1)} %fusion.43, bf16[2048,704]{1,0:T(8,128)(2,1)} %all-gather.6.cloned.1.call-done, f32[128,704]{0,1:T(8,128)S(1)} %fusion.62), kind=kOutput, calls=%fused_computation.45 | convolution fusion | flops 739000320 | bytes 7176192 | tf_op jit(solution)/shard_map/dot_general | solution.py:95
  274.2 4.0 %all-to-all-start.2 = ((bf16[4,128,512]{2,1,0:T(8,128)(2,1)}), bf16[4,128,512]{2,1,0:T(8,128)(2,1)S(1)}, u32[]{:S(2)}, u32[]{:S(2)}) async-start(bf16[4,128,512]{2,1,0:T(8,128)(2,1)} %bitcast.126), calls=%async_computation.2 | async-start | bytes 1048576 | tf_op jit(solution)/shard_map/all_to_all | solution.py:67
  278.2 4.6 %convolution_convert_fusion.2 = bf16[1024,512]{1,0:T(8,128)(2,1)} fusion(bf16[1024,1408]{0,1:T(8,128)(2,1)} %bitcast.28, bf16[1,1408,512]{2,1,0:T(8,128)(2,1)S(1)} %copy-done), kind=kOutput, calls=%fused_computation.46 | convolution fusion | flops 1476919296 | bytes 5373952 | tf_op jit(solution)/shard_map/dot_general | solution.py:78
  282.8 4.4 %all-to-all-done.2 = bf16[4,128,512]{2,1,0:T(8,128)(2,1)S(1)} async-done(((bf16[4,128,512]{2,1,0:T(8,128)(2,1)}), bf16[4,128,512]{2,1,0:T(8,128)(2,1)S(1)}, u32[]{:S(2)}, u32[]{:S(2)}) %all-to-all-start.2) | async-done | bytes 524320 | tf_op jit(solution)/shard_map/all_to_all | solution.py:67
  287.2 7.6 %all-to-all-start.5 = ((bf16[64,16,512]{2,1,0:T(8,128)(2,1)}), bf16[64,16,512]{2,1,0:T(8,128)(2,1)S(1)}, u32[]{:S(2)}, u32[]{:S(2)}) async-start(bf16[64,16,512]{2,1,0:T(8,128)(2,1)} %bitcast.163), calls=%async_computation.5 | async-start | bytes 2097152 | tf_op jit(solution)/shard_map/all_to_all | solution.py:80
  295.9 26.9 %all-to-all-done.5 = bf16[64,16,512]{2,1,0:T(8,128)(2,1)S(1)} async-done(((bf16[64,16,512]{2,1,0:T(8,128)(2,1)}), bf16[64,16,512]{2,1,0:T(8,128)(2,1)S(1)}, u32[]{:S(2)}, u32[]{:S(2)}) %all-to-all-start.5) | async-done | bytes 1048608 | tf_op jit(solution)/shard_map/all_to_all | solution.py:80
  322.8 2.7 gather_fusion.1
  (114 shorter events, 35.0 us)
Async XLA Ops:
  6.5 271.7 %copy-start = (bf16[1,1408,512]{2,1,0:T(8,128)(2,1)S(1)}, bf16[1,1408,512]{2,1,0:T(8,128)(2,1)}, u32[]{:S(2)}) copy-start(bf16[1,1408,512]{2,1,0:T(8,128)(2,1)} %param.32) | copy-start | bytes 4325380
  6.5 201.2 %all-gather.4.cloned.1.call-start = ((), (), s32[]{:S(2)}) async-start(), calls=%async_computation.6 | async-start | bytes 3194880 | tf_op jit(solution)/shard_map/all_gather | solution.py:86
  16.4 1.9 copy-start.1
  16.6 2.6 copy-start.2
  16.6 2.6 copy-start.3
  20.2 1.0 copy-start.4
  20.3 1.0 copy-start.6
  25.5 1.9 copy-start.1
  25.7 2.6 copy-start.2
  25.7 2.6 copy-start.3
  29.4 1.0 copy-start.4
  29.4 1.0 copy-start.6
  35.8 8.3 %copy-start.8 = (s32[128,6]{0,1:T(8,128)S(1)}, s32[128,6]{0,1:T(8,128)}, u32[]{:S(2)}) copy-start(s32[128,6]{0,1:T(8,128)} %param.28) | copy-start | bytes 9220
  38.6 18.1 %all-to-all-start = ((f32[4,128,512]{2,1,0:T(8,128)}), f32[4,128,512]{2,1,0:T(8,128)S(1)}, u32[]{:S(2)}, u32[]{:S(2)}) async-start(f32[4,128,512]{2,1,0:T(8,128)} %convolution_bitcast_fusion), calls=%async_computation | async-start | bytes 2097152 | tf_op jit(solution)/shard_map/all_to_all | solution.py:67
  43.4 25.9 %copy-start.7 = (f32[2048]{0:T(1024)S(1)}, f32[2048]{0:T(1024)}, u32[]{:S(2)}) copy-start(f32[2048]{0:T(1024)} %param.27) | copy-start | bytes 24580
  43.4 167.6 %all-gather.6.cloned.1.call-start = ((), (), s32[]{:S(2)}) async-start(), calls=%async_computation.7 | async-start | bytes 3194880 | tf_op jit(solution)/shard_map/all_gather | solution.py:91
  58.6 10.4 %all-to-all-start.1 = ((bf16[4,128,512]{1,2,0:T(8,128)(2,1)}), bf16[4,128,512]{1,2,0:T(8,128)(2,1)S(1)}, u32[]{:S(2)}, u32[]{:S(2)}) async-start(bf16[4,128,512]{1,2,0:T(8,128)(2,1)} %broadcast_in_dim.54), calls=%async_computation.1 | async-start | bytes 1048576 | tf_op jit(solution)/shard_map/all_to_all | solution.py:56
  72.9 119.8 %all-to-all-start.3 = ((bf16[64,16,2048]{2,1,0:T(8,128)(2,1)}), bf16[64,16,2048]{2,1,0:T(8,128)(2,1)}, u32[]{:S(2)}, u32[]{:S(2)}) async-start(bf16[64,16,2048]{2,1,0:T(8,128)(2,1)} %bitcast.159), calls=%async_computation.3 | async-start | bytes 8388608 | tf_op jit(solution)/shard_map/all_to_all | solution.py:162
  89.2 178.0 %all-gather.8.cloned.1.call-start = ((), (), s32[]{:S(2)}) async-start(), calls=%async_computation.8 | async-start | bytes 3194880 | tf_op jit(solution)/shard_map/all_gather | solution.py:97
  192.7 4.4 %copy-start.10 = (bf16[1,2048,352]{1,2,0:T(8,128)(2,1)S(1)}, bf16[1,2048,352]{1,2,0:T(8,128)(2,1)}, u32[]{:S(2)}) copy-start(bf16[1,2048,352]{1,2,0:T(8,128)(2,1)} %param.31) | copy-start | bytes 4325380
  203.2 71.1 %all-to-all-start.4 = ((bf16[4,1024,352]{1,2,0:T(8,128)(2,1)}), bf16[4,1024,352]{1,2,0:T(8,128)(2,1)}, u32[]{:S(2)}, u32[]{:S(2)}) async-start(bf16[4,1024,352]{1,2,0:T(8,128)(2,1)} %broadcast_in_dim.55), calls=%async_computation.4 | async-start | bytes 5767168 | tf_op jit(solution)/shard_map/all_to_all | solution.py:56
  274.2 13.0 %all-to-all-start.2 = ((bf16[4,128,512]{2,1,0:T(8,128)(2,1)}), bf16[4,128,512]{2,1,0:T(8,128)(2,1)S(1)}, u32[]{:S(2)}, u32[]{:S(2)}) async-start(bf16[4,128,512]{2,1,0:T(8,128)(2,1)} %bitcast.126), calls=%async_computation.2 | async-start | bytes 1048576 | tf_op jit(solution)/shard_map/all_to_all | solution.py:67
  278.2 16.8 %copy-start.9 = (f32[128,6]{0,1:T(8,128)S(1)}, f32[128,6]{0,1:T(8,128)}, u32[]{:S(2)}) copy-start(f32[128,6]{0,1:T(8,128)} %param.29) | copy-start | bytes 9220
  287.2 35.6 %all-to-all-start.5 = ((bf16[64,16,512]{2,1,0:T(8,128)(2,1)}), bf16[64,16,512]{2,1,0:T(8,128)(2,1)S(1)}, u32[]{:S(2)}, u32[]{:S(2)}) async-start(bf16[64,16,512]{2,1,0:T(8,128)(2,1)} %bitcast.163), calls=%async_computation.5 | async-start | bytes 2097152 | tf_op jit(solution)/shard_map/all_to_all | solution.py:80
  (4 other events, 2.6 us)
Sparse Core Ops, SparseCore 0:
  10.1 82.5 all-gather.3
  95.5 89.2 all-gather.5
  187.6 79.5 all-gather.7
where the time goes:
time: 336 us; the launch traced here: 335 us
  waiting for transfers between devices  208 us (62%)
  starting transfers between devices  41 us (12%)
  matrix products  33.6 us (10%)
  local copies, waits for them, and re-layouts  26.5 us (8%)
  between operations  13.4 us (4%)
  other arithmetic  12 us (4%)
    all_to_all x1, waiting for transfers between devices, on_device(): lax.all_to_all(buffer, 'dp', split_axis=0, concat_axis=0, tiled=True)  103 us
    all_gather x1, waiting for transfers between devices, shared_experts(): lax.all_gather(shared_down, 'dp', axis=1, tiled=True)  56.2 us
    all_to_all x1, waiting for transfers between devices, run_experts(): lax.all_to_all(outputs, 'dp', split_axis=0, concat_axis=0, tiled=True)  26.9 us
    all_to_all x1, starting transfers between devices, on_device(): lax.all_to_all(buffer, 'dp', split_axis=0, concat_axis=0, tiled=True)  16.3 us
    all_to_all x2, waiting for transfers between devices, scatter_sum_mp(): lax.all_to_all(blocks, 'mp', split_axis=0, concat_axis=0, tiled=True)  14.4 us
    all_to_all x2, starting transfers between devices, scatter_sum_mp(): lax.all_to_all(blocks, 'mp', split_axis=0, concat_axis=0, tiled=True)  8.82 us
    all_to_all x2, starting transfers between devices, gather_mp(): lax.all_to_all(copies, 'mp', split_axis=0, concat_axis=0, tiled=True)  8.07 us
    all_to_all x1, starting transfers between devices, run_experts(): lax.all_to_all(outputs, 'dp', split_axis=0, concat_axis=0, tiled=True)  7.56 us
  transfers between devices with their start and end apart: 9, of which 6 were waited for; matrix products, arithmetic and copies ran while one was open for 19% of the time, Pallas kernels for 0%

commit v1 on v0

--- a/solution.py
+++ b/solution.py
@@ -94,7 +94,9 @@
     shared_hidden = (jax.nn.silu(gate_total) * up_total).astype(jnp.bfloat16)
     terms = jnp.dot(
         shared_hidden,
-        lax.all_gather(shared_down, "dp", axis=1, tiled=True),
+        jnp.concatenate(
+            lax.all_to_all(jnp.stack([shared_down] * lax.axis_size("dp")), "dp", 0, 0), axis=1
+        ),
         preferred_element_type=jnp.float32,
     )
     return scatter_sum_mp(terms.astype(jnp.bfloat16))

time: 336 us -> 383 us (1.14)
  waiting for transfers between devices: 208 us -> 242 us
  starting transfers between devices: 41 us -> 51.5 us
    all_to_all x0 -> x1, waiting for transfers between devices: none -> 68.5 us  [shared_experts(): lax.all_to_all(jnp.stack([shared_down] * lax.axis_size('dp')), 'dp', 0, 0)]
    all_gather x1 -> x0, waiting for transfers between devices: 56.2 us -> none  [shared_experts(): lax.all_gather(shared_down, 'dp', axis=1, tiled=True)]
    all_to_all x2, waiting for transfers between devices: 6.02 us -> 26.3 us  [gather_mp(): lax.all_to_all(copies, 'mp', split_axis=0, concat_axis=0, tiled=True)]
    all_to_all x0 -> x1, starting transfers between devices: none -> 7.34 us  [shared_experts(): lax.all_to_all(jnp.stack([shared_down] * lax.axis_size('dp')), 'dp', 0, 0)]
  transfers between devices with their start and end apart: 9 -> 9, of which waited for: 6 -> 8; matrix products, arithmetic and copies ran while one was open for 19% -> 8% of each run, Pallas kernels for 0% -> 0%
where the time goes in v1:
time: 383 us; the launch traced here: 381 us
  waiting for transfers between devices  242 us (63%)
  starting transfers between devices  51.5 us (13%)
  matrix products  33.6 us (9%)
  local copies, waits for them, and re-layouts  28.5 us (7%)
  between operations  13.7 us (4%)
  other arithmetic  12 us (3%)
    all_to_all x1, waiting for transfers between devices, on_device(): lax.all_to_all(buffer, 'dp', split_axis=0, concat_axis=0, tiled=True)  103 us
    all_to_all x1, waiting for transfers between devices, shared_experts(): lax.all_to_all(jnp.stack([shared_down] * lax.axis_size('dp')), 'dp', 0, 0)  68.5 us
    all_to_all x1, waiting for transfers between devices, run_experts(): lax.all_to_all(outputs, 'dp', split_axis=0, concat_axis=0, tiled=True)  26.9 us
    all_to_all x2, waiting for transfers between devices, gather_mp(): lax.all_to_all(copies, 'mp', split_axis=0, concat_axis=0, tiled=True)  26.3 us
    all_to_all x1, starting transfers between devices, on_device(): lax.all_to_all(buffer, 'dp', split_axis=0, concat_axis=0, tiled=True)  16.4 us
    all_to_all x2, waiting for transfers between devices, scatter_sum_mp(): lax.all_to_all(blocks, 'mp', split_axis=0, concat_axis=0, tiled=True)  13 us
    all_to_all x1, starting transfers between devices, run_experts(): lax.all_to_all(outputs, 'dp', split_axis=0, concat_axis=0, tiled=True)  11.2 us
    all_to_all x2, starting transfers between devices, scatter_sum_mp(): lax.all_to_all(blocks, 'mp', split_axis=0, concat_axis=0, tiled=True)  8.31 us
  transfers between devices with their start and end apart: 9, of which 8 were waited for; matrix products, arithmetic and copies ran while one was open for 8% of the time, Pallas kernels for 0%

profile of v1, /device:TPU:1, one launch (start us, length us, event | category | flops | bytes accessed | tf_op | source)
XLA Modules:
  0.0 381.4 jit_solution(15175374437302636974)
XLA Ops:
  12.3 18.3 %while.10 = (s32[]{:T(128)}, bf16[2,256,128]{2,1,0:T(8,128)(2,1)}, s32[2]{0:T(128)}, bf16[2,256,128]{2,1,0:T(8,128)(2,1)}, s32[2,32]{1,0:T(2,128)}, /*index=5*/b...) while((s32[]{:T(128)}, bf16[2,256,128]{2,1,0:T(8,128)(2,1)}, ...), condition=%wide.region_5.6_spmd, body=%wide.region_0.5_spmd.sunk | while | flops 554947200 | bytes 25811812 | solution.py:48
  13.0 2.7 gather_fusion
  32.3 2.9 copy.63
  35.2 2.7 convolution_bitcast_fusion
  37.9 4.8 %all-to-all-start = ((f32[4,128,512]{2,1,0:T(8,128)}), f32[4,128,512]{2,1,0:T(8,128)S(1)}, u32[]{:S(2)}, u32[]{:S(2)}) async-start(f32[4,128,512]{2,1,0:T(8,128)} %convolution_bitcast_fusion), calls=%async_computation | async-start | bytes 2097152 | tf_op jit(solution)/shard_map/all_to_all | solution.py:67
  45.3 10.7 %all-to-all-done = f32[4,128,512]{2,1,0:T(8,128)S(1)} async-done(((f32[4,128,512]{2,1,0:T(8,128)}), f32[4,128,512]{2,1,0:T(8,128)S(1)}, u32[]{:S(2)}, u32[]{:S(2)}) %all-to-all-start) | async-done | bytes 1048608 | tf_op jit(solution)/shard_map/all_to_all | solution.py:67
  58.0 3.5 all-to-all-start.1
  62.3 6.0 %all-to-all-done.1 = bf16[4,128,512]{1,2,0:T(8,128)(2,1)S(1)} async-done(((bf16[4,128,512]{1,2,0:T(8,128)(2,1)}), bf16[4,128,512]{1,2,0:T(8,128)(2,1)S(1)}, u32[]{:S(2)}, u32[]{:S(2)}) %all-to-all-start.1) | async-done | bytes 524320 | tf_op jit(solution)/shard_map/all_to_all | solution.py:56
  69.0 3.3 convolution_convert_fusion
  72.3 16.4 %all-to-all-start.4 = ((bf16[64,16,2048]{2,1,0:T(8,128)(2,1)}), bf16[64,16,2048]{2,1,0:T(8,128)(2,1)}, u32[]{:S(2)}, u32[]{:S(2)}) async-start(bf16[64,16,2048]{2,1,0:T(8,128)(2,1)} %bitcast.162), calls=%async_computation.4 | async-start | bytes 8388608 | tf_op jit(solution)/shard_map/all_to_all | solution.py:164
  89.4 102.9 %all-to-all-done.4 = bf16[64,16,2048]{2,1,0:T(8,128)(2,1)} async-done(((bf16[64,16,2048]{2,1,0:T(8,128)(2,1)}), bf16[64,16,2048]{2,1,0:T(8,128)(2,1)}, u32[]{:S(2)}, u32[]{:S(2)}) %all-to-all-start.4) | async-done | bytes 4194336 | tf_op jit(solution)/shard_map/all_to_all | solution.py:164
  194.3 7.3 %all-to-all-start.2 = ((bf16[64,704,32]{1,2,0:T(8,128)(2,1)}), bf16[64,704,32]{1,2,0:T(8,128)(2,1)}, u32[]{:S(2)}, u32[]{:S(2)}) async-start(bf16[64,704,32]{1,2,0:T(8,128)(2,1)} %stack.2), calls=%async_computation.2 | async-start | bytes 6291456 | tf_op jit(solution)/shard_map/all_to_all | solution.py:98
  202.4 4.4 %fusion.36 = f32[1024,352]{0,1:T(8,128)S(1)} fusion(bf16[1024,2048]{1,0:T(8,128)(2,1)} %bitcast.26, bf16[1,2048,352]{1,2,0:T(8,128)(2,1)} %param.30), kind=kOutput, calls=%fused_computation.50 | convolution fusion | flops 1476395008 | bytes 7077888 | tf_op jit(solution)/shard_map/dot_general | solution.py:74
  206.8 4.0 %fusion.38 = bf16[1024,352]{0,1:T(8,128)(2,1)S(1)} fusion(bf16[1024,2048]{1,0:T(8,128)(2,1)} %bitcast.26, bf16[1,2048,352]{1,2,0:T(8,128)(2,1)S(1)} %copy-done.11, f32[1024,352]{0,1:T(8,128)S(1)} %fusion.36), kind=kOutput, calls=%fused_computation.52 | convolution fusion | flops 1478557696 | bytes 7798784 | tf_op jit(solution)/shard_map/dot_general | solution.py:75
  210.9 68.5 %all-to-all-done.2 = bf16[64,704,32]{1,2,0:T(8,128)(2,1)} async-done(((bf16[64,704,32]{1,2,0:T(8,128)(2,1)}), bf16[64,704,32]{1,2,0:T(8,128)(2,1)}, u32[]{:S(2)}, u32[]{:S(2)}) %all-to-all-start.2) | async-done | bytes 2883616 | tf_op jit(solution)/shard_map/all_to_all | solution.py:98
  281.3 4.6 %all-to-all-start.5 = ((bf16[4,1024,352]{1,2,0:T(8,128)(2,1)}), bf16[4,1024,352]{1,2,0:T(8,128)(2,1)}, u32[]{:S(2)}, u32[]{:S(2)}) async-start(bf16[4,1024,352]{1,2,0:T(8,128)(2,1)} %broadcast_in_dim.55), calls=%async_computation.5 | async-start | bytes 5767168 | tf_op jit(solution)/shard_map/all_to_all | solution.py:56
  285.9 3.2 fusion.62
  289.2 2.9 all-gather.5.cloned.1.call-done
  292.0 6.2 %convolution_convert_fusion.1 = bf16[128,2048]{1,0:T(8,128)(2,1)S(1)} fusion(bf16[704,2048]{0,1:T(8,128)(2,1)} %bitcast.22, bf16[128,2048]{0,1:T(8,128)(2,1)S(1)} %fusion.43, bf16[2048,704]{1,0:T(8,128)(2,1)} %all-gather.5.cloned.1.call-done, f32[128,704]{0,1:T(8,128)S(1)} %fusion.62), kind=kOutput, calls=%fused_computation.45 | convolution fusion | flops 739000320 | bytes 7176192 | tf_op jit(solution)/shard_map/dot_general | solution.py:95
  299.1 20.3 %all-to-all-done.5 = bf16[4,1024,352]{1,2,0:T(8,128)(2,1)} async-done(((bf16[4,1024,352]{1,2,0:T(8,128)(2,1)}), bf16[4,1024,352]{1,2,0:T(8,128)(2,1)}, u32[]{:S(2)}, u32[]{:S(2)}) %all-to-all-start.5) | async-done | bytes 2883616 | tf_op jit(solution)/shard_map/all_to_all | solution.py:56
  319.4 3.5 all-to-all-start.3
  322.9 4.6 %convolution_convert_fusion.2 = bf16[1024,512]{1,0:T(8,128)(2,1)} fusion(bf16[1024,1408]{0,1:T(8,128)(2,1)} %bitcast.30, bf16[1,1408,512]{2,1,0:T(8,128)(2,1)S(1)} %copy-done), kind=kOutput, calls=%fused_computation.46 | convolution fusion | flops 1476919296 | bytes 5373952 | tf_op jit(solution)/shard_map/dot_general | solution.py:78
  329.8 11.2 %all-to-all-start.6 = ((bf16[64,16,512]{2,1,0:T(8,128)(2,1)}), bf16[64,16,512]{2,1,0:T(8,128)(2,1)S(1)}, u32[]{:S(2)}, u32[]{:S(2)}) async-start(bf16[64,16,512]{2,1,0:T(8,128)(2,1)} %bitcast.166), calls=%async_computation.6 | async-start | bytes 2097152 | tf_op jit(solution)/shard_map/all_to_all | solution.py:80
  342.0 26.9 %all-to-all-done.6 = bf16[64,16,512]{2,1,0:T(8,128)(2,1)S(1)} async-done(((bf16[64,16,512]{2,1,0:T(8,128)(2,1)}), bf16[64,16,512]{2,1,0:T(8,128)(2,1)S(1)}, u32[]{:S(2)}, u32[]{:S(2)}) %all-to-all-start.6) | async-done | bytes 1048608 | tf_op jit(solution)/shard_map/all_to_all | solution.py:80
  (116 shorter events, 44.0 us)
Async XLA Ops:
  6.5 316.3 %copy-start = (bf16[1,1408,512]{2,1,0:T(8,128)(2,1)S(1)}, bf16[1,1408,512]{2,1,0:T(8,128)(2,1)}, u32[]{:S(2)}) copy-start(bf16[1,1408,512]{2,1,0:T(8,128)(2,1)} %param.32) | copy-start | bytes 4325380
  15.7 1.9 copy-start.1
  15.9 2.6 copy-start.2
  15.9 2.6 copy-start.3
  19.6 1.0 copy-start.4
  19.6 1.0 copy-start.7
  24.8 1.9 copy-start.1
  25.0 2.6 copy-start.2
  25.0 2.6 copy-start.3
  28.7 1.0 copy-start.7
  35.2 7.6 %copy-start.9 = (s32[128,6]{0,1:T(8,128)S(1)}, s32[128,6]{0,1:T(8,128)}, u32[]{:S(2)}) copy-start(s32[128,6]{0,1:T(8,128)} %param.28) | copy-start | bytes 9220
  37.9 18.1 %all-to-all-start = ((f32[4,128,512]{2,1,0:T(8,128)}), f32[4,128,512]{2,1,0:T(8,128)S(1)}, u32[]{:S(2)}, u32[]{:S(2)}) async-start(f32[4,128,512]{2,1,0:T(8,128)} %convolution_bitcast_fusion), calls=%async_computation | async-start | bytes 2097152 | tf_op jit(solution)/shard_map/all_to_all | solution.py:67
  42.7 25.9 %copy-start.8 = (f32[2048]{0:T(1024)S(1)}, f32[2048]{0:T(1024)}, u32[]{:S(2)}) copy-start(f32[2048]{0:T(1024)} %param.27) | copy-start | bytes 24580
  58.0 10.4 %all-to-all-start.1 = ((bf16[4,128,512]{1,2,0:T(8,128)(2,1)}), bf16[4,128,512]{1,2,0:T(8,128)(2,1)S(1)}, u32[]{:S(2)}, u32[]{:S(2)}) async-start(bf16[4,128,512]{1,2,0:T(8,128)(2,1)} %broadcast_in_dim.54), calls=%async_computation.1 | async-start | bytes 1048576 | tf_op jit(solution)/shard_map/all_to_all | solution.py:56
  72.3 120.0 %copy-start.6 = (bf16[704,32]{0,1:T(8,128)(2,1)S(1)}, bf16[704,32]{0,1:T(8,128)(2,1)}, u32[]{:S(2)}) copy-start(bf16[704,32]{0,1:T(8,128)(2,1)} %param.35) | copy-start | bytes 135172
  72.3 120.0 %all-to-all-start.4 = ((bf16[64,16,2048]{2,1,0:T(8,128)(2,1)}), bf16[64,16,2048]{2,1,0:T(8,128)(2,1)}, u32[]{:S(2)}, u32[]{:S(2)}) async-start(bf16[64,16,2048]{2,1,0:T(8,128)(2,1)} %bitcast.162), calls=%async_computation.4 | async-start | bytes 8388608 | tf_op jit(solution)/shard_map/all_to_all | solution.py:164
  88.7 197.3 %all-gather.3.cloned.1.call-start = ((), (), s32[]{:S(2)}) async-start(), calls=%async_computation.7 | async-start | bytes 3194880 | tf_op jit(solution)/shard_map/all_gather | solution.py:86
  194.3 85.0 %all-to-all-start.2 = ((bf16[64,704,32]{1,2,0:T(8,128)(2,1)}), bf16[64,704,32]{1,2,0:T(8,128)(2,1)}, u32[]{:S(2)}, u32[]{:S(2)}) async-start(bf16[64,704,32]{1,2,0:T(8,128)(2,1)} %stack.2), calls=%async_computation.2 | async-start | bytes 6291456 | tf_op jit(solution)/shard_map/all_to_all | solution.py:98
  201.6 90.4 %all-gather.5.cloned.1.call-start = ((), (), s32[]{:S(2)}) async-start(), calls=%async_computation.8 | async-start | bytes 3194880 | tf_op jit(solution)/shard_map/all_gather | solution.py:91
  202.4 4.4 %copy-start.11 = (bf16[1,2048,352]{1,2,0:T(8,128)(2,1)S(1)}, bf16[1,2048,352]{1,2,0:T(8,128)(2,1)}, u32[]{:S(2)}) copy-start(bf16[1,2048,352]{1,2,0:T(8,128)(2,1)} %param.31) | copy-start | bytes 4325380
  281.3 38.1 %all-to-all-start.5 = ((bf16[4,1024,352]{1,2,0:T(8,128)(2,1)}), bf16[4,1024,352]{1,2,0:T(8,128)(2,1)}, u32[]{:S(2)}, u32[]{:S(2)}) async-start(bf16[4,1024,352]{1,2,0:T(8,128)(2,1)} %broadcast_in_dim.55), calls=%async_computation.5 | async-start | bytes 5767168 | tf_op jit(solution)/shard_map/all_to_all | solution.py:56
  319.4 10.4 %all-to-all-start.3 = ((bf16[4,128,512]{2,1,0:T(8,128)(2,1)}), bf16[4,128,512]{2,1,0:T(8,128)(2,1)S(1)}, u32[]{:S(2)}, u32[]{:S(2)}) async-start(bf16[4,128,512]{2,1,0:T(8,128)(2,1)} %bitcast.129), calls=%async_computation.3 | async-start | bytes 1048576 | tf_op jit(solution)/shard_map/all_to_all | solution.py:67
  322.9 18.2 %copy-start.10 = (f32[128,6]{0,1:T(8,128)S(1)}, f32[128,6]{0,1:T(8,128)}, u32[]{:S(2)}) copy-start(f32[128,6]{0,1:T(8,128)} %param.29) | copy-start | bytes 9220
  329.8 39.2 %all-to-all-start.6 = ((bf16[64,16,512]{2,1,0:T(8,128)(2,1)}), bf16[64,16,512]{2,1,0:T(8,128)(2,1)S(1)}, u32[]{:S(2)}, u32[]{:S(2)}) async-start(bf16[64,16,512]{2,1,0:T(8,128)(2,1)} %bitcast.166), calls=%async_computation.6 | async-start | bytes 2097152 | tf_op jit(solution)/shard_map/all_to_all | solution.py:80
  (5 other events, 3.6 us)
Sparse Core Ops, SparseCore 0:
  92.3 90.1 all-gather.2
  205.2 86.7 all-gather.4
